TPU v7x, 256 devices: a whole 4x4x8 slice. The times are simulated.
256 devices in a mesh: row: 16 (over x, z_hi, core), col: 4 (over y), rep: 4 (over z_lo).
Axes of the slice: x: 4, y: 4, z: 8 (z_hi: 2, z_lo: 4; z = z_hi * 4 + z_lo), core: 2. Of those that a mesh axis runs over, the one named last changes fastest.
Arguments:
- integrals: bfloat16 [8, 32, 60, 128, 128], P(None, 'row', 'rep', 'col'), may hold values from -0.0625 to 0.0625
- amplitudes: bfloat16 [8, 16, 60, 128, 128], P(None, 'col', 'rep', 'row'), may hold values from -6 to 6
- virt_count: int32 [8], replicated, may hold values from 76 to 128, as said below
- occ_irrep: int32 [60], replicated, may hold values from 0 to 7
Outputs:
- cycle: bfloat16 [8, 32, 128, 16, 128], P('rep', 'row', None, 'col')
Inputs may be any that keep to these rules, and one draw needn't show every extreme that they name: `virt_count`: one irrep has exactly 128 virtual orbitals.
All inputs are finite; a program needn't handle non-finite values.
Results may differ from a plain program's by a relative error of at most 0.001.
Values may be sent and summed in bfloat16 or wider, within the bound.
No kernel may reach another device: no remote copies, remote signals or barrier semaphores. Data moves between devices by JAX's collectives and lax.ppermute only.
A program may use at most 128 MiB of HBM per device.

v0:
```python
import jax
import jax.numpy as jnp
from jax import lax
from jax.sharding import PartitionSpec as P


def contract(w_part, t_part):
    w_full = lax.all_gather(w_part, "col", axis=3, tiled=True)
    return jnp.einsum(
        "gikca,gjkcb->giajb",
        w_full,
        lax.all_gather(t_part, "row", axis=3, tiled=True),
        preferred_element_type=jnp.float32,
    )


def body(integrals, amplitudes, virt_count, occ_irrep):
    ngroup = integrals.shape[0]
    k_local = integrals.shape[2]
    c_local = integrals.shape[3]
    nvirt = integrals.shape[4]
    rep_index = lax.axis_index("rep")
    col_index = lax.axis_index("col")
    occ_local = lax.dynamic_slice_in_dim(occ_irrep, rep_index * k_local, k_local)
    groups = jnp.arange(ngroup, dtype=jnp.int32)
    blocks = jnp.bitwise_xor(groups[:, None], occ_local[None, :])
    onehot = blocks[:, :, None] == groups[None, None, :]
    limit = jnp.sum(jnp.where(onehot, virt_count[None, None, :], 0), axis=2)
    c_global = col_index * c_local + jnp.arange(c_local, dtype=jnp.int32)
    c_live = c_global[None, None, :] < limit[:, :, None]
    places = jnp.arange(nvirt, dtype=jnp.int32)
    a_live = places[None, :] < virt_count[:, None]
    keep = c_live[:, None, :, :, None] & a_live[:, None, None, None, :]
    masked = jnp.where(keep, integrals, jnp.zeros_like(integrals))
    owned = ngroup // lax.axis_size("rep")
    partial_cycle = contract(masked, amplitudes)
    summed = lax.psum_scatter(partial_cycle, "rep", scatter_dimension=0, tiled=True)
    own_counts = lax.dynamic_slice_in_dim(virt_count, rep_index * owned, owned)
    b_live = places[None, :] < own_counts[:, None]
    result = jnp.where(b_live[:, None, None, None, :], summed, jnp.zeros_like(summed))
    return result.astype(jnp.bfloat16)


def solution(mesh):
    return jax.shard_map(
        body,
        mesh=mesh,
        in_specs=(P(None, "row", "rep", "col", None), P(None, "col", "rep", "row", None), P(), P()),
        out_specs=P("rep", "row", None, "col", None),
        check_vma=False,
    )
```

profile of v0, /device:TPU:1, one launch (start us, length us, event | category | flops | bytes accessed | tf_op | source)
XLA Modules:
  0.0 377.3 jit_solution(17503319874373990578)
XLA Ops:
  6.5 0.0 all-gather.3.cloned.1.call-start
  6.5 0.7 iota_compare_fusion.1
  7.3 0.7 dynamic_slice.7
  8.0 0.7 select_reduce_fusion
  8.7 0.1 broadcast_compare_fusion
  8.8 0.8 broadcast_and_fusion
  9.6 3.1 broadcast_select_fusion
  12.7 0.0 all-gather.3.cloned.1.call-update
  12.8 0.0 all-gather.5.cloned.1.call-start
  12.8 0.7 all-gather.5.cloned.1.call-update
  13.5 0.0 copy-start
  13.5 0.0 reduce-scatter.2.cloned.1.call-start
  13.6 84.3 %all-gather.3.cloned.1.call-done = bf16[8,2,15,128,128]{4,3,2,1,0:T(8,128)(2,1)} async-done(((bf16[8,2,15,32,128]{4,3,2,1,0:T(8,128)(2,1)}), bf16[8,2,15,128,128]{4,3,2,1,0:T(8,128)(2,1)}) %all-gather.3.cloned.1.call-update) | async-done | bytes 7864336 | tf_op jit(solution)/shard_map/all_gather | solution.py:8
  97.8 179.9 %all-gather.5.cloned.1.call-done = bf16[8,4,15,128,128]{4,3,2,1,0:T(8,128)(2,1)} async-done(((bf16[8,4,15,8,128]{4,3,2,1,0:T(8,128)(2,1)}), bf16[8,4,15,128,128]{4,3,2,1,0:T(8,128)(2,1)}) %all-gather.5.cloned.1.call-update) | async-done | bytes 15728656 | tf_op jit(solution)/shard_map/all_gather | solution.py:12
  277.7 14.3 %fusion.3 = f32[8,2,128,4,128]{4,2,3,1,0:T(8,128)} fusion(bf16[8,4,15,128,128]{4,3,2,1,0:T(8,128)(2,1)} %all-gather.5.cloned.1.call-done, bf16[8,2,15,128,128]{4,3,2,1,0:T(8,128)(2,1)} %all-gather.3.cloned.1.call-done), kind=kOutput, calls=%fused_computation.3 | convolution fusion | flops 4026531840 | bytes 27787264 | tf_op jit(solution)/shard_map/gikca,gjkcb->giajb/dot_general | solution.py:9
  292.0 0.0 reduce-scatter.2.cloned.1.call-update
  292.1 0.0 copy-done
  292.1 0.1 dynamic_slice.6
  292.2 0.1 iota_compare_fusion.2
  292.2 76.0 %reduce-scatter.2.cloned.1.call-done = f32[2,2,128,4,128]{4,2,3,1,0:T(8,128)} async-done(((f32[8,2,128,4,128]{4,2,3,1,0:T(8,128)}), f32[2,2,128,4,128]{4,2,3,1,0:T(8,128)}) %reduce-scatter.2.cloned.1.call-update) | async-done | bytes 1048592 | tf_op jit(solution)/shard_map/reduce_scatter | solution.py:37
  368.2 1.3 select_convert_fusion
  369.6 1.2 copy.6
  (2 shorter events, 0.0 us)
Async XLA Ops:
  6.5 91.3 %all-gather.3.cloned.1.call-start = ((), (), s32[]{:S(2)}) async-start(), calls=%async_computation.1 | async-start | bytes 9830400 | tf_op jit(solution)/shard_map/all_gather | solution.py:8
  12.8 265.0 %all-gather.5.cloned.1.call-start = ((), (), s32[]{:S(2)}) async-start(), calls=%async_computation.2 | async-start | bytes 16711680 | tf_op jit(solution)/shard_map/all_gather | solution.py:12
  13.5 278.6 %copy-start = (s32[8]{0:T(128)S(1)}, s32[8]{0:T(128)}, u32[]{:S(2)}) copy-start(s32[8]{0:T(128)} %param.6) | copy-start | bytes 100
  13.5 354.7 %reduce-scatter.2.cloned.1.call-start = ((), (), s32[]{:S(2)}) async-start(), calls=%async_computation.3 | async-start | bytes 5242880 | tf_op jit(solution)/shard_map/reduce_scatter | solution.py:37
Sparse Core Ops, SparseCore 0:
  12.9 84.8 all-gather.2
  100.4 177.3 all-gather.4
  292.2 75.9 reduce-scatter.1
where the time goes:
time: 377 us
  waiting for transfers between devices  341 us (90%)
  matrix products  14.3 us (4%)
  between operations  13.2 us (4%)
  other arithmetic  6.86 us (2%)
    all_gather x1, waiting for transfers between devices, contract(): lax.all_gather(t_part, 'row', axis=3, tiled=True)  180 us
    all_gather x1, waiting for transfers between devices, contract(): w_full = lax.all_gather(w_part, 'col', axis=3, tiled=True)  84.3 us
    reduce_scatter x1, waiting for transfers between devices, body(): lax.psum_scatter(partial_cycle, 'rep', scatter_dimension=0, tiled=True)  76 us
    dot_general x1, matrix products, contract(): jnp.einsum('gikca,gjkcb->giajb', w_full, lax.all_gather(t_part, 'row', ax...  14.3 us
  transfers between devices with their start and end apart: 3, of which 3 were waited for; matrix products, arithmetic and copies ran while one was open for 0% of the time, Pallas kernels for 0%

commit v1 on v0

--- a/solution.py
+++ b/solution.py
@@ -5,7 +5,9 @@
 
 
 def contract(w_part, t_part):
-    w_full = lax.all_gather(w_part, "col", axis=3, tiled=True)
+    w_full = jnp.concatenate(
+        lax.all_to_all(jnp.stack([w_part] * lax.axis_size("col")), "col", 0, 0), axis=3
+    )
     return jnp.einsum(
         "gikca,gjkcb->giajb",
         w_full,

time: 377 us -> 290 us (0.77)
  waiting for transfers between devices: 341 us -> 155 us
  blocking collectives: 0 us -> 92 us
  local copies, waits for them, and re-layouts: 2.01 us -> 9.45 us
    all_gather x1, waiting for transfers between devices: 180 us -> 78.4 us  [contract(): lax.all_gather(t_part, 'row', axis=3, tiled=True)]
    all_to_all x0 -> x1, blocking collectives: none -> 92 us  [contract(): lax.all_to_all(jnp.stack([w_part] * lax.axis_size('col')), 'col', 0, 0)]
    all_gather x1 -> x0, waiting for transfers between devices: 84.3 us -> none  [contract(): w_full = lax.all_gather(w_part, 'col', axis=3, tiled=True)]
    all_to_all x0 -> x1, local copies, waits for them, and re-layouts: none -> 5.32 us  [contract(): lax.all_to_all(jnp.stack([w_part] * lax.axis_size('col')), 'col', 0, 0)]
  transfers between devices with their start and end apart: 3 -> 2, of which waited for: 3 -> 2; matrix products, arithmetic and copies ran while one was open for 0% -> 4% of each run, Pallas kernels for 0% -> 0%
where the time goes in v1:
time: 290 us
  waiting for transfers between devices  155 us (53%)
  blocking collectives  92 us (32%)
  matrix products  14.3 us (5%)
  between operations  13.5 us (5%)
  local copies, waits for them, and re-layouts  9.45 us (3%)
  other arithmetic  5.49 us (2%)
    all_to_all x1, blocking collectives, contract(): lax.all_to_all(jnp.stack([w_part] * lax.axis_size('col')), 'col', 0, 0)  92 us
    all_gather x1, waiting for transfers between devices, contract(): lax.all_gather(t_part, 'row', axis=3, tiled=True)  78.4 us
    reduce_scatter x1, waiting for transfers between devices, body(): lax.psum_scatter(partial_cycle, 'rep', scatter_dimension=0, tiled=True)  76 us
    dot_general x1, matrix products, contract(): jnp.einsum('gikca,gjkcb->giajb', w_full, lax.all_gather(t_part, 'row', ax...  14.3 us
  transfers between devices with their start and end apart: 2, of which 2 were waited for; matrix products, arithmetic and copies ran while one was open for 4% of the time, Pallas kernels for 0%

profile of v1, /device:TPU:1, one launch (start us, length us, event | category | flops | bytes accessed | tf_op | source)
XLA Modules:
  0.0 289.9 jit_solution(8959882487910101929)
XLA Ops:
  6.5 0.0 all-gather.2.cloned.1.call-start
  6.5 0.7 all-gather.2.cloned.1.call-update
  7.3 0.0 reduce-scatter.2.cloned.1.call-start
  7.3 0.7 dynamic_slice.7
  8.0 0.7 select_reduce_fusion
  8.8 0.7 iota_compare_fusion.1
  9.5 0.1 broadcast_compare_fusion
  9.6 0.8 broadcast_and_fusion
  10.4 1.7 broadcast_select_fusion
  12.1 2.1 stack.2
  14.3 92.0 %all_to_all.5 = bf16[4,8,2,15,32,128]{5,4,3,2,1,0:T(8,128)(2,1)S(1)} all-to-all(bf16[4,8,2,15,32,128]{5,4,3,2,1,0:T(8,128)(2,1)S(1)} %stack.2), channel_id=1, replica_groups=mesh['row'=16,'col'=4,'rep'=4] {'col'}, dimensions={0} | all-to-all | bytes 15728640 | tf_op jit(solution)/shard_map/all_to_all | solution.py:9
  106.3 5.3 %copy.12 = bf16[4,8,2,15,32,128]{5,4,0,3,2,1:T(8,128)(2,1)} copy(bf16[4,8,2,15,32,128]{5,4,3,2,1,0:T(8,128)(2,1)S(1)} %all_to_all.5) | data formatting | bytes 15728640 | tf_op jit(solution)/shard_map/all_to_all | solution.py:9
  111.6 78.4 %all-gather.2.cloned.1.call-done = bf16[8,4,15,128,128]{4,3,2,1,0:T(8,128)(2,1)} async-done(((bf16[8,4,15,8,128]{4,3,2,1,0:T(8,128)(2,1)}), bf16[8,4,15,128,128]{4,3,2,1,0:T(8,128)(2,1)}) %all-gather.2.cloned.1.call-update) | async-done | bytes 15728656 | tf_op jit(solution)/shard_map/all_gather | solution.py:14
  190.0 0.0 copy-start
  190.0 14.3 %fusion.2 = f32[8,2,128,4,128]{4,2,3,1,0:T(8,128)} fusion(bf16[8,2,15,128,128,1]{4,3,2,5,1,0:T(8,128)(2,1)} %bitcast.18, bf16[8,4,15,128,128]{4,3,2,1,0:T(8,128)(2,1)} %all-gather.2.cloned.1.call-done), kind=kOutput, calls=%fused_computation.2 | convolution fusion | flops 4026531840 | bytes 27787264 | tf_op jit(solution)/shard_map/gikca,gjkcb->giajb/dot_general | solution.py:11
  204.3 0.0 reduce-scatter.2.cloned.1.call-update
  204.3 0.0 copy-done
  204.3 0.1 dynamic_slice.6
  204.4 0.1 iota_compare_fusion.2
  204.5 76.0 %reduce-scatter.2.cloned.1.call-done = f32[2,2,128,4,128]{4,2,3,1,0:T(8,128)} async-done(((f32[8,2,128,4,128]{4,2,3,1,0:T(8,128)}), f32[2,2,128,4,128]{4,2,3,1,0:T(8,128)}) %reduce-scatter.2.cloned.1.call-update) | async-done | bytes 1048592 | tf_op jit(solution)/shard_map/reduce_scatter | solution.py:39
  280.5 1.3 select_convert_fusion
  281.8 1.2 copy.14
  (2 shorter events, 0.0 us)
Async XLA Ops:
  6.5 183.4 %all-gather.2.cloned.1.call-start = ((), (), s32[]{:S(2)}) async-start(), calls=%async_computation.2 | async-start | bytes 16711680 | tf_op jit(solution)/shard_map/all_gather | solution.py:14
  7.3 273.2 %reduce-scatter.2.cloned.1.call-start = ((), (), s32[]{:S(2)}) async-start(), calls=%async_computation.3 | async-start | bytes 5242880 | tf_op jit(solution)/shard_map/reduce_scatter | solution.py:39
  190.0 14.3 %copy-start = (s32[8]{0:T(128)S(1)}, s32[8]{0:T(128)}, u32[]{:S(2)}) copy-start(s32[8]{0:T(128)} %param.6) | copy-start | bytes 100
Sparse Core Ops, SparseCore 0:
  9.9 180.0 all-gather.1
  204.4 76.0 reduce-scatter.1
